TPU v7x, 256 devices: a whole 4x4x8 slice. The times are simulated.
256 devices in a mesh: layer: 32 (over z, x), row: 2 (over core), col: 4 (over y).
Axes of the slice: x: 4, y: 4, z: 8, core: 2. Of those that a mesh axis runs over, the one named last changes fastest.
Arguments:
- left_factor: float32 [2048, 65536], P('row', ('layer', 'col')), may hold values from -6 to 6
- right_factor: float32 [65536, 4096], P(('layer', 'row'), 'col'), may hold values from -0.15625 to 0.15625
- left_pattern: int32 [32, 1024], P('row', ('layer', 'col')), may hold values 0 or 1
- right_pattern: int32 [1024, 64], P(('layer', 'row'), 'col'), may hold values 0 or 1
- product_pattern: int32 [32, 64], P('row', 'col'), may hold values 0 or 1
Outputs:
- product: float32 [2048, 4096], P(('layer', 'row'), 'col')
All inputs are finite; a program needn't handle non-finite values. No bound on the sum of `left_pattern` or of `right_pattern` or of `product_pattern` on one device may be relied on, other than what follows from the above.
Results may differ from a plain program's by a relative error of at most 0.000092.
Values sent between devices are 32-bit elements; how exact they have to be, the bound alone decides.
No kernel may reach another device: no remote copies, remote signals or barrier semaphores. Data moves between devices by JAX's collectives and lax.ppermute only.
A program may use at most 128 MiB of HBM per device.

v0:
```python
import jax
import jax.numpy as jnp
from jax import lax
from jax.sharding import Mesh
from jax.sharding import PartitionSpec as P

BS = 64


def expand(pattern):
    return jnp.repeat(jnp.repeat(pattern.astype(jnp.float32), BS, axis=0), BS, axis=1)


def body(left_factor, right_factor, left_pattern, right_pattern, product_pattern):
    left = left_factor * expand(left_pattern)
    right = right_factor * expand(right_pattern)
    left_whole = lax.all_gather(left, "col", axis=1, tiled=True)
    partial_sum = jnp.dot(
        left_whole,
        lax.all_gather(right, "row", axis=0, tiled=True),
        preferred_element_type=jnp.float32,
        precision=lax.Precision.HIGHEST,
    )
    kept = partial_sum * expand(product_pattern)
    kept = lax.psum_scatter(kept, "lz", scatter_dimension=0, tiled=True)
    return lax.psum_scatter(kept, "lx", scatter_dimension=0, tiled=True)


def solution(mesh):
    n_layer, n_row, n_col = mesh.devices.shape
    n_x = 4 if n_layer % 4 == 0 else 1
    split = Mesh(
        mesh.devices.reshape(n_layer // n_x, n_x, n_row, n_col), ("lz", "lx", "row", "col")
    )
    layer = ("lz", "lx")
    return jax.shard_map(
        body,
        mesh=split,
        in_specs=(
            P("row", (*layer, "col")),
            P((*layer, "row"), "col"),
            P("row", (*layer, "col")),
            P((*layer, "row"), "col"),
            P("row", "col"),
        ),
        out_specs=P((*layer, "row"), "col"),
        check_vma=False,
    )
```

profile of v0, /device:TPU:8, one launch (start us, length us, event | category | flops | bytes accessed | tf_op | source)
XLA Modules:
  0.0 280.0 jit_solution(4011034189807476211)
XLA Ops:
  6.5 0.0 copy-start
  6.5 0.0 all-gather.5.cloned.1.call-start
  6.5 5.4 %copy.9 = f32[1024,1024]{0,1:T(8,128)} copy(f32[1024,1024]{1,0:T(8,128)} %param.6) | data formatting | bytes 8388608 | tf_op args[1]
  11.9 0.0 copy-done
  11.9 0.1 copy.8
  12.0 0.1 broadcast_in_dim.20
  12.1 0.1 reshape.20
  12.2 5.0 %bitcast_multiply_fusion = f32[1024,1024]{0,1:T(8,128)} fusion(f32[1024,1024]{0,1:T(8,128)} %copy.9, f32[1024,16]{0,1:T(8,128)S(1)} %reshape.20), kind=kLoop, calls=%fused_computation | loop fusion | flops 1048576 | bytes 8454144 | tf_op jit(solution)/shard_map/mul | solution.py:16
  17.2 0.0 copy-start.2
  17.2 0.0 all-gather.5.cloned.1.call-update
  17.2 0.0 all-gather.3.cloned.1.call-start
  17.3 1.9 copy.7
  19.2 0.0 copy-done.2
  19.2 0.0 copy-start.1
  19.3 0.1 broadcast_in_dim.18
  19.3 0.1 reshape.18
  19.4 1.5 bitcast_multiply_fusion.1
  21.0 0.0 all-gather.3.cloned.1.call-update
  21.0 0.0 reduce-scatter.3.cloned.1.call-start
  21.0 0.0 copy-done.1
  21.0 0.1 copy.10
  21.1 0.1 broadcast_in_dim.22
  21.2 0.1 reshape.22
  21.3 2.5 broadcast_in_dim.23
  23.8 5.4 %copy.11 = f32[1024,1024]{1,0:T(8,128)} copy(f32[1024,1024]{0,1:T(8,128)} %bitcast.13) | data formatting | bytes 8388608 | tf_op jit(solution)/shard_map/reshape | solution.py:11
  29.2 16.3 %all-gather.5.cloned.1.call-done = f32[2048,1024]{0,1:T(8,128)} async-done(((f32[1024,1024]{0,1:T(8,128)}), f32[2048,1024]{0,1:T(8,128)}) %all-gather.5.cloned.1.call-update) | async-done | bytes 8388624 | tf_op jit(solution)/shard_map/all_gather | solution.py:20
  45.5 88.7 %all-gather.3.cloned.1.call-done = f32[1024,2048]{0,1:T(8,128)} async-done(((f32[1024,512]{0,1:T(8,128)}), f32[1024,2048]{0,1:T(8,128)}) %all-gather.3.cloned.1.call-update) | async-done | bytes 8388624 | tf_op jit(solution)/shard_map/all_gather | solution.py:17
  134.2 57.5 %convolution_multiply_fusion = f32[1024,1024]{1,0:T(8,128)} fusion(f32[1024,1024]{1,0:T(8,128)} %copy.11, f32[1024,2048]{0,1:T(8,128)} %all-gather.3.cloned.1.call-done, f32[2048,1024]{0,1:T(8,128)} %all-gather.5.cloned.1.call-done), kind=kOutput, calls=%fused_computation.1 | convolution fusion | flops 25770852352 | bytes 25165824 | tf_op jit(solution)/shard_map/dot_general | solution.py:18
  191.7 0.0 reduce-scatter.3.cloned.1.call-update
  191.7 0.0 reduce-scatter.5.cloned.1.call-start
  191.8 56.4 %reduce-scatter.3.cloned.1.call-done = f32[128,1024]{1,0:T(8,128)} async-done(((f32[1024,1024]{1,0:T(8,128)}), f32[128,1024]{1,0:T(8,128)}) %reduce-scatter.3.cloned.1.call-update) | async-done | bytes 524304 | tf_op jit(solution)/shard_map/reduce_scatter | solution.py:25
  248.2 0.0 reduce-scatter.5.cloned.1.call-update
  248.2 25.2 %reduce-scatter.5.cloned.1.call-done = f32[32,1024]{1,0:T(8,128)} async-done(((f32[128,1024]{1,0:T(8,128)}), f32[32,1024]{1,0:T(8,128)}) %reduce-scatter.5.cloned.1.call-update) | async-done | bytes 131088 | tf_op jit(solution)/shard_map/reduce_scatter | solution.py:26
  (3 shorter events, 0.0 us)
Async XLA Ops:
  6.5 5.4 %copy-start = (s32[16,16]{1,0:T(8,128)S(1)}, s32[16,16]{1,0:T(8,128)}, u32[]{:S(2)}) copy-start(s32[16,16]{1,0:T(8,128)} %param.8) | copy-start | bytes 3076
  6.5 38.9 %all-gather.5.cloned.1.call-start = ((), (), s32[]{:S(2)}) async-start(), calls=%async_computation.3 | async-start | bytes 12582912 | tf_op jit(solution)/shard_map/all_gather | solution.py:20
  17.2 2.0 copy-start.2
  17.2 117.0 %all-gather.3.cloned.1.call-start = ((), (), s32[]{:S(2)}) async-start(), calls=%async_computation.2 | async-start | bytes 10485760 | tf_op jit(solution)/shard_map/all_gather | solution.py:17
  19.2 1.8 copy-start.1
  21.0 227.2 %reduce-scatter.3.cloned.1.call-start = ((), (), s32[]{:S(2)}) async-start(), calls=%async_computation.4 | async-start | bytes 4718592 | tf_op jit(solution)/shard_map/reduce_scatter | solution.py:25
  191.7 81.7 %reduce-scatter.5.cloned.1.call-start = ((), (), s32[]{:S(2)}) async-start(), calls=%async_computation.5 | async-start | bytes 655360 | tf_op jit(solution)/shard_map/reduce_scatter | solution.py:26
Sparse Core Ops, SparseCore 0:
  17.4 28.0 all-gather.4
  47.3 86.8 all-gather.2
  191.8 56.3 reduce-scatter.2
  250.6 22.7 reduce-scatter.4
where the time goes:
time: 280 us
  waiting for transfers between devices  187 us (67%)
  matrix products  57.5 us (21%)
  local copies, waits for them, and re-layouts  15.9 us (6%)
  between operations  13.2 us (5%)
  other arithmetic  6.55 us (2%)
    all_gather x1, waiting for transfers between devices, body(): left_whole = lax.all_gather(left, 'col', axis=1, tiled=True)  88.7 us
    dot_general x1, matrix products, body(): jnp.dot(left_whole, lax.all_gather(right, 'row', axis=0, tiled=True), pre...  57.5 us
    reduce_scatter x1, waiting for transfers between devices, body(): kept = lax.psum_scatter(kept, 'lz', scatter_dimension=0, tiled=True)  56.4 us
    reduce_scatter x1, waiting for transfers between devices, body(): return lax.psum_scatter(kept, 'lx', scatter_dimension=0, tiled=True)  25.2 us
    all_gather x1, waiting for transfers between devices, body(): lax.all_gather(right, 'row', axis=0, tiled=True)  16.3 us
    unnamed x8, local copies, waits for them, and re-layouts  7.33 us
  transfers between devices with their start and end apart: 4, of which 4 were waited for; matrix products, arithmetic and copies ran while one was open for 4% of the time, Pallas kernels for 0%

commit v1 on v0

--- a/solution.py
+++ b/solution.py
@@ -15,9 +15,16 @@
     left = left_factor * expand(left_pattern)
     right = right_factor * expand(right_pattern)
     left_whole = lax.all_gather(left, "col", axis=1, tiled=True)
+
+    def steps_all_produce(block_here, across):
+        arr_next = tuple((block_here for _ in range(lax.axis_size(across))))
+        known = jnp.stack(arr_next)
+        w2 = lax.all_to_all(known, across, split_axis=0, concat_axis=0)
+        return jnp.concatenate(w2, axis=0)
+
     partial_sum = jnp.dot(
         left_whole,
-        lax.all_gather(right, "row", axis=0, tiled=True),
+        steps_all_produce(right, "row"),
         preferred_element_type=jnp.float32,
         precision=lax.Precision.HIGHEST,
     )

time: 280 us -> 220 us (0.79)
  waiting for transfers between devices: 187 us -> 133 us
  matrix products: 57.5 us -> 31.9 us
  local copies, waits for them, and re-layouts: 15.9 us -> 24.6 us
  starting transfers between devices: 0.13 us -> 7.75 us
    all_gather x1, waiting for transfers between devices: 88.7 us -> 51.4 us  [body(): left_whole = lax.all_gather(left, 'col', axis=1, tiled=True)]
    dot_general x1, matrix products: 57.5 us -> 31.9 us  [body(): jnp.dot(left_whole, steps_all_produce(right, 'row'), preferred_element_ty...]
    all_gather x1 -> x0, waiting for transfers between devices: 16.3 us -> none  [body(): lax.all_gather(right, 'row', axis=0, tiled=True)]
    all_to_all x0 -> x1, local copies, waits for them, and re-layouts: none -> 8.75 us  [steps_all_produce(): w2 = lax.all_to_all(known, across, split_axis=0, concat_axis=0)]
    all_to_all x0 -> x1, starting transfers between devices: none -> 7.67 us  [steps_all_produce(): w2 = lax.all_to_all(known, across, split_axis=0, concat_axis=0)]
    another operation x0 -> x1, other arithmetic: none -> 4.29 us  [steps_all_produce(): known = jnp.stack(arr_next)]
  transfers between devices with their start and end apart: 4 -> 4, of which waited for: 4 -> 3; matrix products, arithmetic and copies ran while one was open for 4% -> 13% of each run, Pallas kernels for 0% -> 0%
where the time goes in v1:
time: 220 us; the launch traced here: 219 us
  waiting for transfers between devices  133 us (60%)
  matrix products  31.9 us (14%)
  local copies, waits for them, and re-layouts  24.6 us (11%)
  between operations  13.2 us (6%)
  other arithmetic  8.5 us (4%)
  starting transfers between devices  7.75 us (4%)
    reduce_scatter x1, waiting for transfers between devices, body(): kept = lax.psum_scatter(kept, 'lz', scatter_dimension=0, tiled=True)  56.4 us
    all_gather x1, waiting for transfers between devices, body(): left_whole = lax.all_gather(left, 'col', axis=1, tiled=True)  51.4 us
    dot_general x1, matrix products, body(): jnp.dot(left_whole, steps_all_produce(right, 'row'), preferred_element_ty...  31.9 us
    reduce_scatter x1, waiting for transfers between devices, body(): return lax.psum_scatter(kept, 'lx', scatter_dimension=0, tiled=True)  25.3 us
    all_to_all x1, local copies, waits for them, and re-layouts, steps_all_produce(): w2 = lax.all_to_all(known, across, split_axis=0, concat_axis=0)  8.75 us
    all_to_all x1, starting transfers between devices, steps_all_produce(): w2 = lax.all_to_all(known, across, split_axis=0, concat_axis=0)  7.67 us
    unnamed x8, local copies, waits for them, and re-layouts  7.32 us
    reshape x1, local copies, waits for them, and re-layouts, expand(): jnp.repeat(jnp.repeat(pattern.astype(jnp.float32), BS, axis=0), BS, axis=1)  5.4 us
  transfers between devices with their start and end apart: 4, of which 3 were waited for; matrix products, arithmetic and copies ran while one was open for 13% of the time, Pallas kernels for 0%

profile of v1, /device:TPU:8, one launch (start us, length us, event | category | flops | bytes accessed | tf_op | source)
XLA Modules:
  0.0 219.2 jit_solution(13788924196487662262)
XLA Ops:
  6.5 0.0 copy-start.2
  6.5 0.0 all-gather.2.cloned.1.call-start
  6.5 1.9 copy.12
  8.5 0.0 copy-done.2
  8.5 0.1 broadcast_in_dim.18
  8.6 0.1 reshape.21
  8.7 1.5 bitcast_multiply_fusion.1
  10.2 0.0 all-gather.2.cloned.1.call-update
  10.2 0.0 copy-start
  10.2 5.4 %copy.14 = f32[1024,1024]{0,1:T(8,128)} copy(f32[1024,1024]{1,0:T(8,128)} %param.6) | data formatting | bytes 8388608 | tf_op args[1]
  15.6 0.0 copy-done
  15.6 0.1 copy.13
  15.7 0.1 broadcast_in_dim.20
  15.8 0.1 reshape.23
  15.9 2.7 %bitcast_multiply_fusion = f32[1024,1024]{0,1:T(8,128)S(1)} fusion(f32[1024,1024]{0,1:T(8,128)} %copy.14, f32[1024,16]{0,1:T(8,128)S(1)} %reshape.23), kind=kLoop, calls=%fused_computation.1 | loop fusion | flops 1048576 | bytes 8454144 | tf_op jit(solution)/shard_map/mul | solution.py:16
  18.6 4.3 %pad_maximum_fusion = f32[2,1024,1024]{1,2,0:T(8,128)} fusion(f32[1,1024,1024]{1,2,0:T(8,128)S(1)} %bitcast.15), kind=kLoop, calls=%fused_computation | loop fusion | flops 2097152 | bytes 12582912 | tf_op jit(solution)/shard_map/stack | solution.py:21
  22.9 0.0 copy-start.1
  22.9 7.7 %all-to-all-start = ((f32[2,1024,1024]{1,2,0:T(8,128)}), f32[2,1024,1024]{1,2,0:T(8,128)}, u32[]{:S(2)}, u32[]{:S(2)}) async-start(f32[2,1024,1024]{1,2,0:T(8,128)} %pad_maximum_fusion), calls=%async_computation | async-start | bytes 16777216 | tf_op jit(solution)/shard_map/all_to_all | solution.py:22
  30.5 0.0 reduce-scatter.3.cloned.1.call-start
  30.6 0.0 copy-done.1
  30.6 0.1 copy.16
  30.7 0.1 broadcast_in_dim.22
  30.8 0.1 reshape.26
  30.9 2.5 %broadcast_in_dim.23 = f32[1024,16,64]{0,2,1:T(8,128)} broadcast(f32[1024,16]{0,1:T(8,128)S(1)} %reshape.26), dimensions={0,1} | broadcast | bytes 4259840 | tf_op jit(solution)/shard_map/broadcast_in_dim | solution.py:11
  33.3 5.4 %copy.17 = f32[1024,1024]{1,0:T(8,128)} copy(f32[1024,1024]{0,1:T(8,128)} %bitcast.16) | data formatting | bytes 8388608 | tf_op jit(solution)/shard_map/reshape | solution.py:11
  38.7 0.0 all-to-all-done
  38.7 8.7 %copy.15 = f32[2,1024,1024]{2,1,0:T(8,128)} copy(f32[2,1024,1024]{1,2,0:T(8,128)} %all-to-all-done) | data formatting | bytes 16777216 | tf_op jit(solution)/shard_map/all_to_all | solution.py:22
  47.5 51.4 %all-gather.2.cloned.1.call-done = f32[1024,2048]{0,1:T(8,128)} async-done(((f32[1024,512]{0,1:T(8,128)}), f32[1024,2048]{0,1:T(8,128)}) %all-gather.2.cloned.1.call-update) | async-done | bytes 8388624 | tf_op jit(solution)/shard_map/all_gather | solution.py:17
  98.9 31.9 %convolution_multiply_fusion = f32[1024,1024]{1,0:T(8,128)} fusion(f32[1024,1024]{1,0:T(8,128)} %copy.17, f32[1024,2048]{0,1:T(8,128)} %all-gather.2.cloned.1.call-done, f32[2048,1024]{1,0:T(8,128)} %bitcast.17), kind=kOutput, calls=%fused_computation.2 | convolution fusion | flops 25770852352 | bytes 25165824 | tf_op jit(solution)/shard_map/dot_general | solution.py:25
  130.8 0.0 reduce-scatter.3.cloned.1.call-update
  130.8 0.0 reduce-scatter.5.cloned.1.call-start
  130.9 56.4 %reduce-scatter.3.cloned.1.call-done = f32[128,1024]{1,0:T(8,128)} async-done(((f32[1024,1024]{1,0:T(8,128)}), f32[128,1024]{1,0:T(8,128)}) %reduce-scatter.3.cloned.1.call-update) | async-done | bytes 524304 | tf_op jit(solution)/shard_map/reduce_scatter | solution.py:32
  187.3 0.0 reduce-scatter.5.cloned.1.call-update
  187.3 25.3 %reduce-scatter.5.cloned.1.call-done = f32[32,1024]{1,0:T(8,128)} async-done(((f32[128,1024]{1,0:T(8,128)}), f32[32,1024]{1,0:T(8,128)}) %reduce-scatter.5.cloned.1.call-update) | async-done | bytes 131088 | tf_op jit(solution)/shard_map/reduce_scatter | solution.py:33
  (3 shorter events, 0.0 us)
Async XLA Ops:
  6.5 1.9 copy-start.2
  6.5 92.3 %all-gather.2.cloned.1.call-start = ((), (), s32[]{:S(2)}) async-start(), calls=%async_computation.3 | async-start | bytes 10485760 | tf_op jit(solution)/shard_map/all_gather | solution.py:17
  10.2 5.4 %copy-start = (s32[16,16]{1,0:T(8,128)S(1)}, s32[16,16]{1,0:T(8,128)}, u32[]{:S(2)}) copy-start(s32[16,16]{1,0:T(8,128)} %param.8) | copy-start | bytes 3076
  22.9 7.7 %copy-start.1 = (s32[16,16]{1,0:T(8,128)S(1)}, s32[16,16]{1,0:T(8,128)}, u32[]{:S(2)}) copy-start(s32[16,16]{1,0:T(8,128)} %param.9) | copy-start | bytes 3076
  22.9 15.9 %all-to-all-start = ((f32[2,1024,1024]{1,2,0:T(8,128)}), f32[2,1024,1024]{1,2,0:T(8,128)}, u32[]{:S(2)}, u32[]{:S(2)}) async-start(f32[2,1024,1024]{1,2,0:T(8,128)} %pad_maximum_fusion), calls=%async_computation | async-start | bytes 16777216 | tf_op jit(solution)/shard_map/all_to_all | solution.py:22
  30.5 156.8 %reduce-scatter.3.cloned.1.call-start = ((), (), s32[]{:S(2)}) async-start(), calls=%async_computation.4 | async-start | bytes 4718592 | tf_op jit(solution)/shard_map/reduce_scatter | solution.py:32
  130.8 81.8 %reduce-scatter.5.cloned.1.call-start = ((), (), s32[]{:S(2)}) async-start(), calls=%async_computation.5 | async-start | bytes 655360 | tf_op jit(solution)/shard_map/reduce_scatter | solution.py:33
Sparse Core Ops, SparseCore 0:
  10.3 88.4 all-gather.1
  131.0 56.3 reduce-scatter.2
  189.9 22.7 reduce-scatter.4

commit v2 on v0

--- a/solution.py
+++ b/solution.py
@@ -14,7 +14,22 @@
 def body(left_factor, right_factor, left_pattern, right_pattern, product_pattern):
     left = left_factor * expand(left_pattern)
     right = right_factor * expand(right_pattern)
-    left_whole = lax.all_gather(left, "col", axis=1, tiled=True)
+    ways, here, step = (lax.axis_size("col"), lax.axis_index("col"), left.shape[1])
+    shape = [n * ways if d == 1 else n for d, n in enumerate(left.shape)]
+    left_whole = lax.dynamic_update_slice_in_dim(
+        jnp.zeros(shape, left.dtype), left, here * step, axis=1
+    )
+    going_up = going_down = left
+    for far in range(1, ways // 2 + 1):
+        going_up = lax.ppermute(going_up, "col", [(d, (d + 1) % ways) for d in range(ways)])
+        left_whole = lax.dynamic_update_slice_in_dim(
+            left_whole, going_up, (here - far) % ways * step, axis=1
+        )
+        if 2 * far < ways:
+            going_down = lax.ppermute(going_down, "col", [(d, (d - 1) % ways) for d in range(ways)])
+            left_whole = lax.dynamic_update_slice_in_dim(
+                left_whole, going_down, (here + far) % ways * step, axis=1
+            )
     partial_sum = jnp.dot(
         left_whole,
         lax.all_gather(right, "row", axis=0, tiled=True),

time: 280 us -> 271 us (0.968)
  waiting for transfers between devices: 187 us -> 162 us
  local copies, waits for them, and re-layouts: 15.9 us -> 28 us
  starting transfers between devices: 0.13 us -> 3.82 us
    all_gather x1 -> x0, waiting for transfers between devices: 88.7 us -> none  [body(): left_whole = lax.all_gather(left, 'col', axis=1, tiled=True)]
    ppermute x0 -> x3, waiting for transfers between devices: none -> 77.6 us  [the longest x2 77.6 us: body(): lax.ppermute(going_up, 'col', [(d, (d + 1) % ways) for d in range(ways)])]
    all_gather x1, waiting for transfers between devices: 16.3 us -> 0.01 us  [body(): lax.all_gather(right, 'row', axis=0, tiled=True)]
    dynamic_update_slice x0 -> x3, local copies, waits for them, and re-layouts: none -> 7.81 us  [the longest x2 4.64 us: body(): lax.dynamic_update_slice_in_dim(left_whole, going_up, (here - far) % ways...]
    ppermute x0 -> x3, starting transfers between devices: none -> 3.74 us  [the longest x2 3.15 us: body(): lax.ppermute(going_up, 'col', [(d, (d + 1) % ways) for d in range(ways)])]
    unnamed x8 -> x10, local copies, waits for them, and re-layouts: 7.33 us -> 10.6 us
  transfers between devices with their start and end apart: 4 -> 6, of which waited for: 4 -> 4; matrix products, arithmetic and copies ran while one was open for 4% -> 8% of each run, Pallas kernels for 0% -> 0%
where the time goes in v2:
time: 271 us
  waiting for transfers between devices  162 us (60%)
  matrix products  57.5 us (21%)
  local copies, waits for them, and re-layouts  28 us (10%)
  between operations  13.2 us (5%)
  other arithmetic  6.85 us (3%)
  starting transfers between devices  3.82 us (1%)
    ppermute x2, waiting for transfers between devices, body(): lax.ppermute(going_up, 'col', [(d, (d + 1) % ways) for d in range(ways)])  77.6 us
    reduce_scatter x1, waiting for transfers between devices, body(): kept = lax.psum_scatter(kept, 'lz', scatter_dimension=0, tiled=True)  58.5 us
    dot_general x1, matrix products, body(): jnp.dot(left_whole, lax.all_gather(right, 'row', axis=0, tiled=True), pre...  57.5 us
    reduce_scatter x1, waiting for transfers between devices, body(): return lax.psum_scatter(kept, 'lx', scatter_dimension=0, tiled=True)  25.3 us
    unnamed x10, local copies, waits for them, and re-layouts  10.6 us
  transfers between devices with their start and end apart: 6, of which 4 were waited for; matrix products, arithmetic and copies ran while one was open for 8% of the time, Pallas kernels for 0%

profile of v2, /device:TPU:8, one launch (start us, length us, event | category | flops | bytes accessed | tf_op | source)
XLA Modules:
  0.0 270.8 jit_solution(4007710700812664650)
XLA Ops:
  6.5 0.0 copy-start.1
  6.5 0.0 all-gather.2.cloned.1.call-start
  6.5 5.4 %copy.9 = f32[1024,1024]{0,1:T(8,128)} copy(f32[1024,1024]{1,0:T(8,128)} %param.6) | data formatting | bytes 8388608 | tf_op args[1]
  11.9 0.0 copy-done.1
  11.9 0.1 copy.8
  12.0 0.1 broadcast_in_dim.24
  12.1 0.1 reshape.20
  12.2 5.0 %bitcast_multiply_fusion = f32[1024,1024]{0,1:T(8,128)} fusion(f32[1024,1024]{0,1:T(8,128)} %copy.9, f32[1024,16]{0,1:T(8,128)S(1)} %reshape.20), kind=kLoop, calls=%fused_computation | loop fusion | flops 1048576 | bytes 8454144 | tf_op jit(solution)/shard_map/mul | solution.py:16
  17.2 0.0 copy-start.3
  17.2 0.0 all-gather.2.cloned.1.call-update
  17.2 0.0 reduce-scatter.3.cloned.1.call-start
  17.3 1.9 copy.7
  19.2 0.0 copy-done.3
  19.2 0.1 broadcast_in_dim.22
  19.3 0.1 reshape.18
  19.4 1.1 broadcast_in_dim.21
  20.5 0.0 copy-start.2
  20.5 1.8 constant_dynamic-update-slice_fusion.3
  22.3 0.0 copy-start
  22.3 3.2 %copy-done = f32[1024,2048]{0,1:T(8,128)} copy-done((f32[1024,2048]{0,1:T(8,128)}, f32[1024,2048]{0,1:T(8,128)S(1)}, u32[]{:S(2)}) %copy-start) | copy-done | bytes 8388632
  25.5 1.6 collective-permute-start
  27.1 0.6 collective-permute-start.1
  27.7 45.4 %collective-permute-done = f32[1024,512]{0,1:T(8,128)S(1)} collective-permute-done((f32[1024,512]{0,1:T(8,128)}, f32[1024,512]{0,1:T(8,128)S(1)}, u32[]{:S(2)}, u32[]{:S(2)}) %collective-permute-start) | collective-permute-done | bytes 2097184 | tf_op jit(solution)/shard_map/ppermute | solution.py:24
  73.1 1.6 collective-permute-start.2
  74.7 0.0 copy-done.2
  74.7 0.1 copy.10
  74.8 0.1 broadcast_in_dim.26
  74.9 0.1 reshape.22
  75.0 2.5 broadcast_in_dim.27
  77.5 5.4 %copy.11 = f32[1024,1024]{1,0:T(8,128)} copy(f32[1024,1024]{0,1:T(8,128)} %bitcast.13) | data formatting | bytes 8388608 | tf_op jit(solution)/shard_map/reshape | solution.py:11
  82.9 1.5 constant_dynamic-update-slice_fusion.2
  84.4 0.0 collective-permute-done.1
  84.4 3.2 %constant_dynamic-update-slice_fusion.1 = f32[1024,2048]{0,1:T(8,128)} fusion(f32[1024,2048]{0,1:T(8,128)} %constant_dynamic-update-slice_fusion.2, f32[1024,512]{0,1:T(8,128)} %collective-permute-done.1, s32[]{:T(128)S(6)} %select_n.31), kind=kLoop, calls=%fused_computation.4 | loop fusion | bytes 4194308 | tf_op jit(solution)/shard_map/dynamic_update_slice | solution.py:30
  87.5 32.2 %collective-permute-done.2 = f32[1024,512]{0,1:T(8,128)} collective-permute-done((f32[1024,512]{0,1:T(8,128)S(1)}, f32[1024,512]{0,1:T(8,128)}, u32[]{:S(2)}, u32[]{:S(2)}) %collective-permute-start.2) | collective-permute-done | bytes 2097184 | tf_op jit(solution)/shard_map/ppermute | solution.py:24
  119.7 3.1 %constant_dynamic-update-slice_fusion = f32[1024,2048]{0,1:T(8,128)} fusion(f32[1024,2048]{0,1:T(8,128)} %constant_dynamic-update-slice_fusion.1, f32[1024,512]{0,1:T(8,128)} %collective-permute-done.2, s32[]{:T(128)S(6)} %select_n.33), kind=kLoop, calls=%fused_computation.3 | loop fusion | bytes 4194308 | tf_op jit(solution)/shard_map/dynamic_update_slice | solution.py:25
  122.9 0.0 all-gather.2.cloned.1.call-done
  122.9 57.5 %convolution_multiply_fusion = f32[1024,1024]{1,0:T(8,128)} fusion(f32[1024,1024]{1,0:T(8,128)} %copy.11, f32[1024,2048]{0,1:T(8,128)} %constant_dynamic-update-slice_fusion, f32[2048,1024]{0,1:T(8,128)} %all-gather.2.cloned.1.call-done), kind=kOutput, calls=%fused_computation.1 | convolution fusion | flops 25770852352 | bytes 25165824 | tf_op jit(solution)/shard_map/dot_general | solution.py:33
  180.4 0.0 reduce-scatter.3.cloned.1.call-update
  180.4 0.0 reduce-scatter.5.cloned.1.call-start
  180.4 58.5 %reduce-scatter.3.cloned.1.call-done = f32[128,1024]{1,0:T(8,128)} async-done(((f32[1024,1024]{1,0:T(8,128)}), f32[128,1024]{1,0:T(8,128)}) %reduce-scatter.3.cloned.1.call-update) | async-done | bytes 524304 | tf_op jit(solution)/shard_map/reduce_scatter | solution.py:40
  238.9 0.0 reduce-scatter.5.cloned.1.call-update
  239.0 25.3 %reduce-scatter.5.cloned.1.call-done = f32[32,1024]{1,0:T(8,128)} async-done(((f32[128,1024]{1,0:T(8,128)}), f32[32,1024]{1,0:T(8,128)}) %reduce-scatter.5.cloned.1.call-update) | async-done | bytes 131088 | tf_op jit(solution)/shard_map/reduce_scatter | solution.py:41
  (3 shorter events, 0.0 us)
Async XLA Ops:
  6.5 5.4 %copy-start.1 = (s32[16,16]{1,0:T(8,128)S(1)}, s32[16,16]{1,0:T(8,128)}, u32[]{:S(2)}) copy-start(s32[16,16]{1,0:T(8,128)} %param.8) | copy-start | bytes 3076
  6.5 116.3 %all-gather.2.cloned.1.call-start = ((), (), s32[]{:S(2)}) async-start(), calls=%async_computation.2 | async-start | bytes 12582912 | tf_op jit(solution)/shard_map/all_gather | solution.py:35
  17.2 2.0 copy-start.3
  17.2 221.7 %reduce-scatter.3.cloned.1.call-start = ((), (), s32[]{:S(2)}) async-start(), calls=%async_computation.3 | async-start | bytes 4718592 | tf_op jit(solution)/shard_map/reduce_scatter | solution.py:40
  20.5 54.2 %copy-start.2 = (s32[16,16]{1,0:T(8,128)S(1)}, s32[16,16]{1,0:T(8,128)}, u32[]{:S(2)}) copy-start(s32[16,16]{1,0:T(8,128)} %param.9) | copy-start | bytes 3076
  22.3 3.2 %copy-start = (f32[1024,2048]{0,1:T(8,128)}, f32[1024,2048]{0,1:T(8,128)S(1)}, u32[]{:S(2)}) copy-start(f32[1024,2048]{0,1:T(8,128)S(1)} %get-tuple-element.5) | copy-start | bytes 25165828
  25.5 47.6 %collective-permute-start = (f32[1024,512]{0,1:T(8,128)}, f32[1024,512]{0,1:T(8,128)S(1)}, u32[]{:S(2)}, u32[]{:S(2)}) collective-permute-start(f32[1024,512]{0,1:T(8,128)} %get-tuple-element.6), channel_id=1, source_target_pairs={{0,1},{1,2},{2,3},{3,0},{4,5},{5,6},{6,7},{7,4},{8,9},{9,10},{10,1... | collective-permute-start | bytes 6291464 | tf_op jit(solution)/shard_map/ppermute | solution.py:24
  27.1 57.2 %collective-permute-start.1 = (f32[1024,512]{0,1:T(8,128)}, f32[1024,512]{0,1:T(8,128)}, u32[]{:S(2)}, u32[]{:S(2)}) collective-permute-start(f32[1024,512]{0,1:T(8,128)} %get-tuple-element.6), channel_id=1, source_target_pairs={{0,3},{1,0},{2,1},{3,2},{4,7},{5,4},{6,5},{7,6},{8,11},{9,8},{10,9... | collective-permute-start | bytes 6291464 | tf_op jit(solution)/shard_map/ppermute | solution.py:29
  73.1 46.6 %collective-permute-start.2 = (f32[1024,512]{0,1:T(8,128)S(1)}, f32[1024,512]{0,1:T(8,128)}, u32[]{:S(2)}, u32[]{:S(2)}) collective-permute-start(f32[1024,512]{0,1:T(8,128)S(1)} %collective-permute-done), channel_id=1, source_target_pairs={{0,1},{1,2},{2,3},{3,0},{4,5},{5,6},{6,7},{7,4},{8,9},{9,10},{10,1... | collective-permute-start | bytes 6291464 | tf_op jit(solution)/shard_map/ppermute | solution.py:24
  180.4 83.9 %reduce-scatter.5.cloned.1.call-start = ((), (), s32[]{:S(2)}) async-start(), calls=%async_computation.4 | async-start | bytes 655360 | tf_op jit(solution)/shard_map/reduce_scatter | solution.py:41
Sparse Core Ops, SparseCore 0:
  17.4 28.0 all-gather.1
  180.5 58.4 reduce-scatter.2
  241.5 22.7 reduce-scatter.4
